TPU v7x, 128 devices: a whole 4x4x4 slice. The times are simulated.
128 devices in a mesh: req: 32 (over x, y, core), tp: 4 (over z).
Axes of the slice: x: 4, y: 4, z: 4, core: 2. Of those that a mesh axis runs over, the one named last changes fastest.
Arguments:
- stream: bfloat16 [64, 64, 3584], P('req'), may hold values from -40 to 40
- queries: bfloat16 [64, 64, 3584], P('req', None, 'tp'), may hold values from -4 to 4
- key_new: bfloat16 [64, 64, 3584], P('req', None, 'tp'), may hold values from -18 to 18
- value_new: bfloat16 [64, 64, 3584], P('req', None, 'tp'), may hold values from -6 to 6
- cache_key: bfloat16 [64, 1024, 3584], P('req', None, 'tp'), may hold values from -5 to 5
- cache_value: bfloat16 [64, 1024, 3584], P('req', None, 'tp'), may hold values from -6 to 6
- cache_length: int32 [64], P('req'), may hold values from 64 to 1024, as said below
- parents: int32 [64, 64], P('req'), may hold values from -1 to 62, as said below
- accept: int32 [64, 8, 64], P('req'), may hold values from 0 to 1, as said below
- out_weight: bfloat16 [3584, 3584], P('tp'), may hold values from -0.75 to 0.75
- norm_gain: float32 [3584], replicated, may hold values from 0.1 to 1.9
- head_weight: bfloat16 [32000, 3584], P('req'), may hold values from -1 to 1
- candidate: int32 [64, 64], replicated, may hold values from 0 to 31999
- dealing: int32 [64], replicated, may hold values from 0 to 63, each once
Outputs:
- target_logprob: float32 [64, 64], P('req')
- accepted_state: bfloat16 [64, 8, 3584], P('req', None, 'tp')
Inputs may be any that keep to these rules, and one draw needn't show every extreme that they name: `cache_length`: every cache holds at least 64 live positions; in every draw some slot's cache is full. `parents`: node 0 is the root with parent -1; node t > 0 lies at depth (t - 1) // 9 + 1 and its parent lies one depth above it. `accept`: row a of a slot's matrix is one-hot on the node at depth a of the accepted path, which runs from the root down the slot's tree to some node; rows past the path's end are zero; in every draw some path ends at the deepest level.
All inputs are finite; a program needn't handle non-finite values.
Results may differ from a plain program's by a relative error of at most 0.012.
Values may be sent and summed in bfloat16 or wider, within the bound.
No kernel may reach another device: no remote copies, remote signals or barrier semaphores. Data moves between devices by JAX's collectives and lax.ppermute only.
A program may use at most 192 MiB of HBM per device.

v0:
```python
import jax
import jax.numpy as jnp
from jax import lax
from jax.sharding import PartitionSpec as P

HD = 224
ACC = 8
EPS = 1e-05
HIGH = lax.Precision.HIGHEST
block_limit = 512


def combined_all(value, axis, join):
    pieces = jax.tree.map(lambda part: lax.all_gather(part, axis), value)
    head = jax.tree.map(lambda part: part[0], pieces)
    tail = jax.tree.map(lambda part: part[1:], pieces)
    subtotal, _ = lax.scan(lambda subtotal, share: (join(subtotal, share), None), head, tail)
    return subtotal


def ancestry(parents):
    node_count = parents.shape[-1]
    node_ids = jnp.arange(node_count, dtype=jnp.int32)
    stride_map = (parents[..., :, None] == node_ids).astype(jnp.float32)
    reached = jnp.broadcast_to(jnp.eye(node_count, dtype=jnp.float32), stride_map.shape) > 0.5
    for doubling in range((ACC - 1).bit_length()):
        further = lax.optimization_barrier(
            jnp.einsum("rtk,rku->rtu", reached.astype(jnp.float32), stride_map, precision=HIGH)
        )
        reached = jnp.logical_or(reached, further > 0.5)
        stride_map = jnp.einsum("rtk,rku->rtu", stride_map, stride_map, precision=HIGH)
    return reached


def combine_stats(earlier, later):
    joint_max = jnp.maximum(earlier[0], later[0])
    joint_sum = earlier[1] * jnp.exp(earlier[0] - joint_max) + later[1] * jnp.exp(
        later[0] - joint_max
    )
    return (joint_max, joint_sum, earlier[2] + later[2])


def vocab_stats(logits, vocab_ids, wanted, along):
    row_max = jnp.max(logits, axis=along)
    row_sum = jnp.sum(jnp.exp(logits - jnp.expand_dims(row_max, along)), axis=along)
    matches = jnp.expand_dims(vocab_ids, 1 - along) == jnp.expand_dims(wanted, along)
    picked = jnp.sum(jnp.where(matches, logits, 0.0), axis=along)
    return (row_max, row_sum, picked)


def local(
    stream,
    queries,
    key_new,
    value_new,
    cache_key,
    cache_value,
    cache_length,
    parents,
    accept,
    out_weight,
    norm_gain,
    head_weight,
    candidate,
    dealing,
):
    slots, tree_size, qwidth = queries.shape
    model_width = stream.shape[2]
    heads_loc = qwidth // HD
    n_tp = lax.axis_size("tp")
    n_req = lax.axis_size("req")
    tp_id = lax.axis_index("tp")
    req_id = lax.axis_index("req")
    score_scale = HD ** (-0.5)
    query_rows = queries.reshape(slots, tree_size, heads_loc, HD)
    tree_keys = key_new.reshape(slots, tree_size, heads_loc, HD)
    tree_values = value_new.reshape(slots, tree_size, heads_loc, HD)
    visible = ancestry(parents)
    tree_scores = (
        jnp.einsum("rthd,rkhd->rhtk", query_rows, tree_keys, preferred_element_type=jnp.float32)
        * score_scale
    )
    tree_scores = jnp.where(visible[:, None], tree_scores, -jnp.inf)
    running_max = jnp.max(tree_scores, axis=3)
    weights = jnp.exp(tree_scores - running_max[..., None])
    running_sum = jnp.sum(weights, axis=3)
    running_out = jnp.einsum(
        "rhtk,rkhd->rhtd",
        weights.astype(jnp.bfloat16),
        tree_values,
        preferred_element_type=jnp.float32,
    )
    cache_cap = cache_key.shape[1]
    block_rows = min(block_limit, cache_cap)
    block_count = (jnp.max(cache_length) + block_rows - 1) // block_rows

    def visit_block(block_index, folded):
        old_max, old_sum, old_out = folded
        offset = block_index * block_rows
        past_keys = lax.dynamic_slice_in_dim(cache_key, offset, block_rows, 1).reshape(
            slots, block_rows, heads_loc, HD
        )
        past_values = lax.dynamic_slice_in_dim(cache_value, offset, block_rows, 1).reshape(
            slots, block_rows, heads_loc, HD
        )
        scores = (
            jnp.einsum("rthd,rkhd->rhtk", query_rows, past_keys, preferred_element_type=jnp.float32)
            * score_scale
        )
        live_mask = (offset + jnp.arange(block_rows, dtype=jnp.int32))[None, :] < cache_length[
            :, None
        ]
        scores = jnp.where(live_mask[:, None, None, :], scores, -jnp.inf)
        new_max = jnp.maximum(old_max, jnp.max(scores, axis=3))
        shrink = jnp.exp(old_max - new_max)
        block_weights = jnp.exp(scores - new_max[..., None])
        new_sum = old_sum * shrink + jnp.sum(block_weights, axis=3)
        contribution = lax.optimization_barrier(
            jnp.einsum(
                "rhtk,rkhd->rhtd",
                block_weights.astype(jnp.bfloat16),
                past_values,
                preferred_element_type=jnp.float32,
            )
        )
        new_out = old_out * shrink[..., None] + contribution
        return (new_max, new_sum, new_out)

    running_max, running_sum, running_out = lax.fori_loop(
        0, block_count, visit_block, (running_max, running_sum, running_out)
    )
    attention = (running_out / running_sum[..., None]).astype(jnp.bfloat16)
    attention_rows = attention.transpose(0, 2, 1, 3).reshape(slots * tree_size, qwidth)
    flat_stream = stream.reshape(slots * tree_size, model_width)
    rows_all = slots * tree_size
    quarter = rows_all // n_tp
    dslice = model_width // n_tp
    partial_out = jnp.dot(attention_rows, out_weight, preferred_element_type=jnp.float32)
    summed = lax.psum_scatter(
        partial_out.astype(jnp.bfloat16), "tp", scatter_dimension=1, tiled=True
    ).astype(jnp.float32)
    own_stream = lax.dynamic_slice_in_dim(flat_stream, tp_id * dslice, dslice, 1)
    post_rows = (own_stream.astype(jnp.float32) + summed).astype(jnp.bfloat16)
    post_float = post_rows.astype(jnp.float32)
    square = jnp.sum(post_float * post_float, axis=1)
    energy = lax.psum(square, "tp")
    inverse = lax.rsqrt(energy / model_width + EPS)
    part_gain = lax.dynamic_slice_in_dim(norm_gain, tp_id * dslice, dslice, 0)
    normed_slice = (post_float * inverse[:, None] * part_gain[None, :]).astype(jnp.bfloat16)
    compact = jnp.einsum(
        "sat,std->sad",
        accept.astype(jnp.bfloat16),
        post_rows.reshape(slots, tree_size, dslice),
        preferred_element_type=jnp.float32,
    ).astype(jnp.bfloat16)
    normed = lax.all_to_all(normed_slice, "tp", split_axis=0, concat_axis=1, tiled=True)
    vocab_loc = head_weight.shape[0]
    wanted_rows = lax.dynamic_slice_in_dim(
        candidate.reshape(n_req, rows_all), tp_id * quarter, quarter, 1
    ).reshape(-1)
    vocab_ids = req_id * vocab_loc + jnp.arange(vocab_loc, dtype=jnp.int32)
    logits = lax.dot_general(
        lax.all_gather(normed, "req", axis=0, tiled=True),
        head_weight,
        (((1,), (1,)), ((), ())),
        preferred_element_type=jnp.float32,
    )
    found_stats = vocab_stats(logits, vocab_ids, wanted_rows, 1)
    local_stats = tuple((after_part for after_part in found_stats))
    merged = combined_all((local_stats[0], local_stats[1], local_stats[2]), "req", combine_stats)
    all_stats = (
        lax.all_gather(merged[0], "tp", axis=0, tiled=True),
        lax.all_gather(merged[1], "tp", axis=0, tiled=True),
        lax.all_gather(merged[2], "tp", axis=0, tiled=True),
    )
    row_max, row_sum, picked = tuple(
        (
            member.reshape(n_tp, n_req, quarter).transpose(1, 0, 2).reshape(-1)
            for member in all_stats
        )
    )
    logprob = (picked - row_max - jnp.log(row_sum)).reshape(-1, tree_size)
    own_requests = req_id * slots + jnp.arange(slots, dtype=jnp.int32)
    selector = dealing[None, :] == own_requests[:, None]
    target_logprob = jnp.dot(selector.astype(jnp.float32), logprob, precision=HIGH)
    home_states = lax.all_gather(compact, "req", axis=0, tiled=True)
    accepted_state = jnp.einsum(
        "ks,sad->kad",
        selector.astype(jnp.bfloat16),
        home_states,
        preferred_element_type=jnp.float32,
    ).astype(jnp.bfloat16)
    return (target_logprob, accepted_state)


def solution(mesh):
    placed = (
        P("req", None, None),
        P("req", None, "tp"),
        P("req", None, "tp"),
        P("req", None, "tp"),
        P("req", None, "tp"),
        P("req", None, "tp"),
        P("req"),
        P("req", None),
        P("req", None, None),
        P("tp", None),
        P(),
        P("req", None),
        P(),
        P(),
    )
    return jax.shard_map(
        local,
        mesh=mesh,
        in_specs=placed,
        out_specs=(P("req", None), P("req", None, "tp")),
        check_vma=False,
    )
```

profile of v0, /device:TPU:0, one launch (start us, length us, event | category | flops | bytes accessed | tf_op | source)
XLA Modules:
  0.0 275.6 jit_solution(6451548967636028759)
XLA Ops:
  7.2 1.4 reduce_max.37
  11.9 1.2 reshape.97
  15.1 1.2 reshape.99
  16.9 12.5 %while.28 = (s32[]{:T(128)}, f32[2,4,64]{2,1,0:T(4,128)S(1)}, f32[2,4,64]{2,1,0:T(4,128)S(1)}, f32[2,4,64,224]{3,2,1,0:T(8,128)S(1)}, s32[]{:T(128)}, /*index=5*...) while((s32[]{:T(128)}, f32[2,4,64]{2,1,0:T(4,128)S(1)}, ...), condition=%wide.region_6.7_spmd, body=%wide.region_3.6_spmd.sunk | while | flops 236947968 | bytes 23599292 | solution.py:129
  17.0 4.1 %constant_dynamic-slice_fusion.9 = (bf16[2,512,896]{2,1,0:T(8,128)(2,1)}, bf16[2,512,896]{2,1,0:T(8,128)(2,1)}) fusion(bf16[2,1024,896]{2,1,0:T(8,128)(2,1)} %get-tuple-element.346, s32[]{:T(128)S(6)} %select_n.42, bf16[2,1024,896]{2,1,0:T(8,128)(2,1)} %get-tuple-element.344), kind=kLoop, calls=%fused_computation.13.clone.1 | loop fusion | bytes 7340036 | tf_op jit(solution)/shard_map/while/body/dynamic_slice | solution.py:103
  21.1 2.7 copy.80
  23.9 1.5 fusion.66
  25.8 2.8 copy.81
  30.0 4.0 %convolution_convert_fusion = bf16[128,3584]{1,0:T(8,128)(2,1)S(1)} fusion(bf16[128,896]{1,0:T(8,128)(2,1)S(1)} %reshape.100, bf16[896,3584]{1,0:T(8,128)(2,1)} %param.27), kind=kOutput, calls=%fused_computation.19 | convolution fusion | flops 822542336 | bytes 7569408 | tf_op jit(solution)/shard_map/dot_general | solution.py:138
  34.0 1.3 copy.61
  36.1 37.4 %reduce-scatter.4.cloned.1.call-done = bf16[896,128]{1,0:T(8,128)(2,1)} async-done(((bf16[3584,128]{1,0:T(8,128)(2,1)}), bf16[896,128]{1,0:T(8,128)(2,1)}) %reduce-scatter.4.cloned.1.call-update) | async-done | bytes 229392
  75.7 8.0 %psum.7 = f32[128]{0:T(128)S(1)} all-reduce(f32[128]{0:T(128)S(1)} %get-tuple-element.177), channel_id=1, replica_groups=mesh['req'=32,'tp'=4] {'tp'}, use_global_device_ids=true, to_apply=%region_9.10 | all-reduce | flops 128 | bytes 1024 | tf_op jit(solution)/shard_map/psum | solution.py:146
  83.9 9.3 %all_to_all.19 = bf16[4,32,896]{2,1,0:T(8,128)(2,1)S(1)} all-to-all(bf16[4,32,896]{2,1,0:T(8,128)(2,1)S(1)} %bitcast.79), channel_id=1, replica_groups=mesh['req'=32,'tp'=4] {'tp'}, dimensions={0} | all-to-all | bytes 458752 | tf_op jit(solution)/shard_map/all_to_all | solution.py:156
  94.3 25.4 %all_gather.43 = bf16[64,8,896]{2,1,0:T(8,128)(2,1)S(1)} all-gather(bf16[2,8,896]{2,1,0:T(8,128)(2,1)S(1)} %fusion.8), channel_id=1, replica_groups=mesh['req'=32,'tp'=4] {'req'}, dimensions={0}, use_global_device_ids=true | all-gather | bytes 946176 | tf_op jit(solution)/shard_map/all_gather | solution.py:186
  120.7 23.6 %all-gather.5.cloned.1.call-done = bf16[1024,3584]{1,0:T(8,128)(2,1)} async-done(((bf16[32,3584]{1,0:T(8,128)(2,1)}), bf16[1024,3584]{1,0:T(8,128)(2,1)}) %all-gather.5.cloned.1.call-update) | async-done | bytes 7340048 | tf_op jit(solution)/shard_map/all_gather | solution.py:163
  144.2 12.1 %fusion.36 = (f32[1024]{0:T(1024)S(1)}, f32[1024,1000]{0,1:T(8,128)S(1)}) fusion(bf16[1024,3584]{1,0:T(8,128)(2,1)} %all-gather.5.cloned.1.call-done, bf16[1000,3584]{1,0:T(8,128)(2,1)} %param.29), kind=kOutput, calls=%fused_computation.70 | convolution fusion | flops 7341054976 | bytes 18608128 | tf_op jit(solution)/shard_map/dot_general | solution.py:162
  156.3 1.4 select_reduce_fusion
  157.7 24.1 %all-gather.2 = f32[32768]{0:T(1024)S(1)} all-gather(f32[1024]{0:T(1024)S(1)} %get-tuple-element.139), channel_id=4, replica_groups=mesh['req'=32,'tp'=4] {'req'}, dimensions={0}, use_global_device_ids=true | all-gather | bytes 135168 | tf_op jit(solution)/shard_map/all_gather | solution.py:14
  181.8 22.7 %all-gather = f32[32768]{0:T(1024)S(1)} all-gather(f32[1024]{0:T(1024)S(1)} %get-tuple-element.187), channel_id=2, replica_groups=mesh['req'=32,'tp'=4] {'req'}, dimensions={0}, use_global_device_ids=true | all-gather | bytes 135168 | tf_op jit(solution)/shard_map/all_gather | solution.py:14
  204.5 23.8 %all-gather.1 = f32[32768]{0:T(1024)S(1)} all-gather(f32[1024]{0:T(1024)S(1)} %get-tuple-element.140), channel_id=3, replica_groups=mesh['req'=32,'tp'=4] {'req'}, dimensions={0}, use_global_device_ids=true | all-gather | bytes 135168 | tf_op jit(solution)/shard_map/all_gather | solution.py:14
  228.4 2.8 %while.29 = (s32[]{:T(128)}, f32[1024]{0:T(1024)S(1)}, f32[1024]{0:T(1024)S(1)}, f32[1024]{0:T(1024)S(1)}, f32[31,1024]{1,0:T(8,128)S(1)}, /*index=5*/f32[31,1024]{1,0:T(8,128)S(1)}, f32[31,1024]{1,0:T(8,128)S(1)}, s32[]{:T(128)}) while((s32[]{:T(128)}, f32[1024]{0:T(1024)S(1)}, f32[1024]{0:T(1024)S(1)}, f32[1024]{0:T(1024)S(1)}, ...), condition=%wide.region_14.15_spmd, body=%wide.region_13.14_spmd.sunk | while | flops 7170 | bytes 61541 | solution.py:17
  231.2 12.5 %all_gather.40 = f32[4096]{0:T(1024)S(1)} all-gather(f32[1024]{0:T(1024)S(1)} %get-tuple-element.92), channel_id=1, replica_groups=mesh['req'=32,'tp'=4] {'tp'}, dimensions={0}, use_global_device_ids=true | all-gather | bytes 20480 | tf_op jit(solution)/shard_map/all_gather | solution.py:174
  243.7 12.0 %all_gather.41 = f32[4096]{0:T(1024)S(1)} all-gather(f32[1024]{0:T(1024)S(1)} %get-tuple-element.93), channel_id=1, replica_groups=mesh['req'=32,'tp'=4] {'tp'}, dimensions={0}, use_global_device_ids=true | all-gather | bytes 20480 | tf_op jit(solution)/shard_map/all_gather | solution.py:172
  255.7 12.0 %all_gather.42 = f32[4096]{0:T(1024)S(1)} all-gather(f32[1024]{0:T(1024)S(1)} %get-tuple-element.94), channel_id=1, replica_groups=mesh['req'=32,'tp'=4] {'tp'}, dimensions={0}, use_global_device_ids=true | all-gather | bytes 20480 | tf_op jit(solution)/shard_map/all_gather | solution.py:173
  (189 shorter events, 14.7 us)
Async XLA Ops:
  7.2 9.7 %copy-start.1 = (s32[2]{0:T(128)S(1)}, s32[2]{0:T(128)}, u32[]{:S(2)}) copy-start(s32[2]{0:T(128)} %param.24) | copy-start | bytes 28
  7.2 66.4 %reduce-scatter.4.cloned.1.call-start = ((), (), s32[]{:S(2)}) async-start(), calls=%async_computation.3 | async-start | bytes 1146880
  34.0 60.0 %copy-start = (s32[64,64]{1,0:T(8,128)S(1)}, s32[64,64]{1,0:T(8,128)}, u32[]{:S(2)}) copy-start(s32[64,64]{1,0:T(8,128)} %param.30) | copy-start | bytes 49156
  34.0 60.2 %copy-start.2 = (s32[2,8,64]{2,1,0:T(8,128)S(1)}, s32[2,8,64]{2,1,0:T(8,128)}, u32[]{:S(2)}) copy-start(s32[2,8,64]{2,1,0:T(8,128)} %param.26) | copy-start | bytes 12292
  34.0 85.8 %copy-start.3 = (s32[64]{0:T(128)S(1)}, s32[64]{0:T(128)}, u32[]{:S(2)}) copy-start(s32[64]{0:T(128)} %param.31) | copy-start | bytes 772
  35.3 108.9 %all-gather.5.cloned.1.call-start = ((), (), s32[]{:S(2)}) async-start(), calls=%async_computation.2 | async-start | bytes 7569408 | tf_op jit(solution)/shard_map/all_gather | solution.py:163
Sparse Core Ops, SparseCore 0:
  35.4 38.0 reduce-scatter.3
  94.1 50.1 all-gather.4
where the time goes:
time: 276 us
  blocking collectives  150 us (54%)
  waiting for transfers between devices  61 us (22%)
  matrix products  22.3 us (8%)
  local copies, waits for them, and re-layouts  20.5 us (7%)
  between operations  15 us (5%)
  other arithmetic  5.41 us (2%)
    all_gather x3, blocking collectives, combined_all(): pieces = jax.tree.map(lambda part: lax.all_gather(part, axis), value)  70.6 us
    unnamed x3, waiting for transfers between devices  37.4 us
    all_gather x1, blocking collectives, local(): home_states = lax.all_gather(compact, 'req', axis=0, tiled=True)  25.4 us
    all_gather x1, waiting for transfers between devices, local(): lax.all_gather(normed, 'req', axis=0, tiled=True)  23.6 us
    all_gather x1, blocking collectives, local(): lax.all_gather(merged[2], 'tp', axis=0, tiled=True)  12.5 us
    dot_general x1, matrix products, local(): lax.dot_general(lax.all_gather(normed, 'req', axis=0, tiled=True), head_w...  12.1 us
    all_gather x1, blocking collectives, local(): lax.all_gather(merged[0], 'tp', axis=0, tiled=True)  12 us
    all_gather x1, blocking collectives, local(): lax.all_gather(merged[1], 'tp', axis=0, tiled=True)  12 us
  transfers between devices with their start and end apart: 2, of which 2 were waited for; matrix products, arithmetic and copies ran while one was open for 1% of the time, Pallas kernels for 0%

commit v1 on v0

--- a/solution.py
+++ b/solution.py
@@ -143,7 +143,9 @@
     post_rows = (own_stream.astype(jnp.float32) + summed).astype(jnp.bfloat16)
     post_float = post_rows.astype(jnp.float32)
     square = jnp.sum(post_float * post_float, axis=1)
-    energy = lax.psum(square, "tp")
+    energy = square
+    for hop in (1, 2):
+        energy = energy + lax.ppermute(energy, "tp", [(dev, dev ^ hop) for dev in range(4)])
     inverse = lax.rsqrt(energy / model_width + EPS)
     part_gain = lax.dynamic_slice_in_dim(norm_gain, tp_id * dslice, dslice, 0)
     normed_slice = (post_float * inverse[:, None] * part_gain[None, :]).astype(jnp.bfloat16)

time: 276 us -> 277 us (level)
  blocking collectives: 150 us -> 142 us
  waiting for transfers between devices: 61 us -> 68.2 us
    psum x1 -> x0, blocking collectives: 7.98 us -> none  [local(): energy = lax.psum(square, 'tp')]
    ppermute x0 -> x2, waiting for transfers between devices: none -> 6.39 us  [local(): lax.ppermute(energy, 'tp', [(dev, dev ^ hop) for dev in range(4)])]
  transfers between devices with their start and end apart: 2 -> 4, of which waited for: 2 -> 4; matrix products, arithmetic and copies ran while one was open for 1% -> 1% of each run, Pallas kernels for 0% -> 0%
where the time goes in v1:
time: 277 us; the launch traced here: 276 us
  blocking collectives  142 us (51%)
  waiting for transfers between devices  68.2 us (25%)
  matrix products  22.3 us (8%)
  local copies, waits for them, and re-layouts  20.5 us (7%)
  between operations  15.1 us (5%)
  other arithmetic  5.42 us (2%)
    all_gather x3, blocking collectives, combined_all(): pieces = jax.tree.map(lambda part: lax.all_gather(part, axis), value)  70.6 us
    unnamed x3, waiting for transfers between devices  38.2 us
    all_gather x1, blocking collectives, local(): home_states = lax.all_gather(compact, 'req', axis=0, tiled=True)  25.4 us
    all_gather x1, waiting for transfers between devices, local(): lax.all_gather(normed, 'req', axis=0, tiled=True)  23.6 us
    all_gather x1, blocking collectives, local(): lax.all_gather(merged[2], 'tp', axis=0, tiled=True)  12.5 us
    dot_general x1, matrix products, local(): lax.dot_general(lax.all_gather(normed, 'req', axis=0, tiled=True), head_w...  12.1 us
    all_gather x1, blocking collectives, local(): lax.all_gather(merged[0], 'tp', axis=0, tiled=True)  12 us
    all_gather x1, blocking collectives, local(): lax.all_gather(merged[1], 'tp', axis=0, tiled=True)  12 us
  transfers between devices with their start and end apart: 4, of which 4 were waited for; matrix products, arithmetic and copies ran while one was open for 1% of the time, Pallas kernels for 0%

profile of v1, /device:TPU:0, one launch (start us, length us, event | category | flops | bytes accessed | tf_op | source)
XLA Modules:
  0.0 276.0 jit_solution(9484009583331463496)
XLA Ops:
  7.2 1.4 reduce_max.37
  16.9 12.5 %while.28 = (s32[]{:T(128)}, f32[2,4,64]{2,1,0:T(4,128)S(1)}, f32[2,4,64]{2,1,0:T(4,128)S(1)}, f32[2,4,64,224]{3,2,1,0:T(8,128)S(1)}, s32[]{:T(128)}, /*index=5*...) while((s32[]{:T(128)}, f32[2,4,64]{2,1,0:T(4,128)S(1)}, ...), condition=%wide.region_6.7_spmd, body=%wide.region_3.6_spmd.sunk | while | flops 236947968 | bytes 23599292 | solution.py:129
  17.0 4.1 %constant_dynamic-slice_fusion.9 = (bf16[2,512,896]{2,1,0:T(8,128)(2,1)}, bf16[2,512,896]{2,1,0:T(8,128)(2,1)}) fusion(bf16[2,1024,896]{2,1,0:T(8,128)(2,1)} %get-tuple-element.346, s32[]{:T(128)S(6)} %select_n.42, bf16[2,1024,896]{2,1,0:T(8,128)(2,1)} %get-tuple-element.344), kind=kLoop, calls=%fused_computation.13.clone.1 | loop fusion | bytes 7340036 | tf_op jit(solution)/shard_map/while/body/dynamic_slice | solution.py:103
  21.1 2.7 copy.80
  23.9 1.5 fusion.66
  25.8 2.8 copy.81
  30.0 4.0 %convolution_convert_fusion = bf16[128,3584]{1,0:T(8,128)(2,1)S(1)} fusion(bf16[128,896]{1,0:T(8,128)(2,1)S(1)} %reshape.100, bf16[896,3584]{1,0:T(8,128)(2,1)} %param.27), kind=kOutput, calls=%fused_computation.19 | convolution fusion | flops 822542336 | bytes 7569408 | tf_op jit(solution)/shard_map/dot_general | solution.py:138
  34.0 1.3 copy.61
  35.4 38.2 %reduce-scatter.4.cloned.1.call-done = bf16[896,128]{1,0:T(8,128)(2,1)} async-done(((bf16[3584,128]{1,0:T(8,128)(2,1)}), bf16[896,128]{1,0:T(8,128)(2,1)}) %reduce-scatter.4.cloned.1.call-update) | async-done | bytes 229392
  75.8 3.6 %collective-permute-done = f32[128]{0:T(128)S(1)} collective-permute-done((f32[128]{0:T(128)S(1)}, f32[128]{0:T(128)S(1)}, u32[]{:S(2)}, u32[]{:S(2)}) %collective-permute-start) | collective-permute-done | bytes 544 | tf_op jit(solution)/shard_map/ppermute | solution.py:148
  79.4 1.5 collective-permute-start.1
  81.6 2.8 %collective-permute-done.1 = f32[128]{0:T(128)S(1)} collective-permute-done((f32[128]{0:T(128)S(1)}, f32[128]{0:T(128)S(1)}, u32[]{:S(2)}, u32[]{:S(2)}) %collective-permute-start.1) | collective-permute-done | bytes 544 | tf_op jit(solution)/shard_map/ppermute | solution.py:148
  84.6 9.0 %all_to_all.19 = bf16[4,32,896]{2,1,0:T(8,128)(2,1)S(1)} all-to-all(bf16[4,32,896]{2,1,0:T(8,128)(2,1)S(1)} %bitcast.79), channel_id=1, replica_groups=mesh['req'=32,'tp'=4] {'tp'}, dimensions={0} | all-to-all | bytes 458752 | tf_op jit(solution)/shard_map/all_to_all | solution.py:158
  94.8 25.4 %all_gather.43 = bf16[64,8,896]{2,1,0:T(8,128)(2,1)S(1)} all-gather(bf16[2,8,896]{2,1,0:T(8,128)(2,1)S(1)} %fusion.8), channel_id=1, replica_groups=mesh['req'=32,'tp'=4] {'req'}, dimensions={0}, use_global_device_ids=true | all-gather | bytes 946176 | tf_op jit(solution)/shard_map/all_gather | solution.py:188
  121.1 23.6 %all-gather.5.cloned.1.call-done = bf16[1024,3584]{1,0:T(8,128)(2,1)} async-done(((bf16[32,3584]{1,0:T(8,128)(2,1)}), bf16[1024,3584]{1,0:T(8,128)(2,1)}) %all-gather.5.cloned.1.call-update) | async-done | bytes 7340048 | tf_op jit(solution)/shard_map/all_gather | solution.py:165
  144.7 12.1 %fusion.36 = (f32[1024]{0:T(1024)S(1)}, f32[1024,1000]{0,1:T(8,128)S(1)}) fusion(bf16[1024,3584]{1,0:T(8,128)(2,1)} %all-gather.5.cloned.1.call-done, bf16[1000,3584]{1,0:T(8,128)(2,1)} %param.29), kind=kOutput, calls=%fused_computation.70 | convolution fusion | flops 7341054976 | bytes 18608128 | tf_op jit(solution)/shard_map/dot_general | solution.py:164
  156.7 1.4 select_reduce_fusion
  158.2 24.1 %all-gather.2 = f32[32768]{0:T(1024)S(1)} all-gather(f32[1024]{0:T(1024)S(1)} %get-tuple-element.139), channel_id=4, replica_groups=mesh['req'=32,'tp'=4] {'req'}, dimensions={0}, use_global_device_ids=true | all-gather | bytes 135168 | tf_op jit(solution)/shard_map/all_gather | solution.py:14
  182.2 22.7 %all-gather = f32[32768]{0:T(1024)S(1)} all-gather(f32[1024]{0:T(1024)S(1)} %get-tuple-element.187), channel_id=2, replica_groups=mesh['req'=32,'tp'=4] {'req'}, dimensions={0}, use_global_device_ids=true | all-gather | bytes 135168 | tf_op jit(solution)/shard_map/all_gather | solution.py:14
  204.9 23.8 %all-gather.1 = f32[32768]{0:T(1024)S(1)} all-gather(f32[1024]{0:T(1024)S(1)} %get-tuple-element.140), channel_id=3, replica_groups=mesh['req'=32,'tp'=4] {'req'}, dimensions={0}, use_global_device_ids=true | all-gather | bytes 135168 | tf_op jit(solution)/shard_map/all_gather | solution.py:14
  228.9 2.8 %while.29 = (s32[]{:T(128)}, f32[1024]{0:T(1024)S(1)}, f32[1024]{0:T(1024)S(1)}, f32[1024]{0:T(1024)S(1)}, f32[31,1024]{1,0:T(8,128)S(1)}, /*index=5*/f32[31,1024]{1,0:T(8,128)S(1)}, f32[31,1024]{1,0:T(8,128)S(1)}, s32[]{:T(128)}) while((s32[]{:T(128)}, f32[1024]{0:T(1024)S(1)}, f32[1024]{0:T(1024)S(1)}, f32[1024]{0:T(1024)S(1)}, ...), condition=%wide.region_13.14_spmd, body=%wide.region_12.13_spmd.sunk | while | flops 7170 | bytes 61541 | solution.py:17
  231.7 12.5 %all_gather.40 = f32[4096]{0:T(1024)S(1)} all-gather(f32[1024]{0:T(1024)S(1)} %get-tuple-element.92), channel_id=1, replica_groups=mesh['req'=32,'tp'=4] {'tp'}, dimensions={0}, use_global_device_ids=true | all-gather | bytes 20480 | tf_op jit(solution)/shard_map/all_gather | solution.py:176
  244.2 12.0 %all_gather.41 = f32[4096]{0:T(1024)S(1)} all-gather(f32[1024]{0:T(1024)S(1)} %get-tuple-element.93), channel_id=1, replica_groups=mesh['req'=32,'tp'=4] {'tp'}, dimensions={0}, use_global_device_ids=true | all-gather | bytes 20480 | tf_op jit(solution)/shard_map/all_gather | solution.py:174
  256.2 12.0 %all_gather.42 = f32[4096]{0:T(1024)S(1)} all-gather(f32[1024]{0:T(1024)S(1)} %get-tuple-element.94), channel_id=1, replica_groups=mesh['req'=32,'tp'=4] {'tp'}, dimensions={0}, use_global_device_ids=true | all-gather | bytes 20480 | tf_op jit(solution)/shard_map/all_gather | solution.py:175
  (193 shorter events, 17.2 us)
Async XLA Ops:
  7.2 9.7 %copy-start.1 = (s32[2]{0:T(128)S(1)}, s32[2]{0:T(128)}, u32[]{:S(2)}) copy-start(s32[2]{0:T(128)} %param.24) | copy-start | bytes 28
  7.2 66.4 %reduce-scatter.4.cloned.1.call-start = ((), (), s32[]{:S(2)}) async-start(), calls=%async_computation.3 | async-start | bytes 1146880
  34.0 60.4 %copy-start = (s32[64,64]{1,0:T(8,128)S(1)}, s32[64,64]{1,0:T(8,128)}, u32[]{:S(2)}) copy-start(s32[64,64]{1,0:T(8,128)} %param.30) | copy-start | bytes 49156
  34.0 60.7 %copy-start.2 = (s32[2,8,64]{2,1,0:T(8,128)S(1)}, s32[2,8,64]{2,1,0:T(8,128)}, u32[]{:S(2)}) copy-start(s32[2,8,64]{2,1,0:T(8,128)} %param.26) | copy-start | bytes 12292
  34.0 86.2 %copy-start.3 = (s32[64]{0:T(128)S(1)}, s32[64]{0:T(128)}, u32[]{:S(2)}) copy-start(s32[64]{0:T(128)} %param.31) | copy-start | bytes 772
  35.3 109.4 %all-gather.5.cloned.1.call-start = ((), (), s32[]{:S(2)}) async-start(), calls=%async_computation.2 | async-start | bytes 7569408 | tf_op jit(solution)/shard_map/all_gather | solution.py:165
  75.7 3.6 %collective-permute-start = (f32[128]{0:T(128)S(1)}, f32[128]{0:T(128)S(1)}, u32[]{:S(2)}, u32[]{:S(2)}) collective-permute-start(f32[128]{0:T(128)S(1)} %get-tuple-element.177), channel_id=1, source_target_pairs={{0,1},{1,0},{2,3},{3,2},{4,5},{5,4},{6,7},{7,6},{8,9},{9,8},{10,11... | collective-permute-start | bytes 1544 | tf_op jit(solution)/shard_map/ppermute | solution.py:148
  79.4 5.1 %collective-permute-start.1 = (f32[128]{0:T(128)S(1)}, f32[128]{0:T(128)S(1)}, u32[]{:S(2)}, u32[]{:S(2)}) collective-permute-start(f32[128]{0:T(128)S(1)} %add.85), channel_id=1, source_target_pairs={{0,2},{1,3},{2,0},{3,1},{4,6},{5,7},{6,4},{7,5},{8,10},{9,11},{10,... | collective-permute-start | bytes 1544 | tf_op jit(solution)/shard_map/ppermute | solution.py:148
Sparse Core Ops, SparseCore 0:
  35.4 38.0 reduce-scatter.3
  94.5 50.1 all-gather.4
